TPU v7x, 32 devices: a whole 2x2x4 slice. The times are simulated.
32 devices in a mesh: chain: 2 (over x), ops: 8 (over z, y), sector: 2 (over core).
Axes of the slice: x: 2, y: 2, z: 4, core: 2. Of those that a mesh axis runs over, the one named last changes fastest.
Arguments:
- psi: bfloat16 [2, 8, 384, 384], P('chain', 'sector'), may hold values from -90 to 90
- left_ops: bfloat16 [2, 96, 8, 384, 384], P('chain', 'ops', 'sector'), may hold values from -1 to 2
- right_ops: bfloat16 [2, 96, 8, 384, 384], P('chain', 'ops', 'sector'), may hold values from -1 to 1
- basis: bfloat16 [2, 8, 384, 384], P('chain', 'sector'), may hold values from -0.3125 to 0.3125
- block_dims: int32 [2, 8], P('chain', 'sector'), may hold values from 64 to 384, as said below
Outputs:
- residual: float32 [2, 8, 384, 384], P('chain', 'sector', 'ops')
- thetas: float32 [2, 3], P('chain')
Inputs may be any that keep to these rules, and one draw needn't show every extreme that they name: `block_dims`: each is a multiple of 64; every section has a sector of exactly 384.
All inputs are finite; a program needn't handle non-finite values.
Results may differ from a plain program's by a relative error of at most 0.009.
Values may be sent and summed in bfloat16 or wider, within the bound.
No kernel may reach another device: no remote copies, remote signals or barrier semaphores. Data moves between devices by JAX's collectives and lax.ppermute only.
A program may use at most 128 MiB of HBM per device.

v0:
```python
import jax
import jax.numpy as jnp
from jax import lax
from jax.sharding import PartitionSpec as P

SECTORS = 8
ITERS = 3


def from_behind(block, axis, distance):
    devices = range(lax.axis_size(axis))
    route = [((i - distance) % len(devices), i) for i in devices]
    return lax.ppermute(block, axis, route)


def live_mask(block_dims, block_size):
    index_rows = jnp.arange(block_size, dtype=jnp.int32)
    limits = block_dims[:, :, None, None]
    inside = (index_rows[None, None, :, None] < limits) & (index_rows[None, None, None, :] < limits)
    return inside.astype(jnp.float32)


def quotient(vector_rows, sigma_rows):
    correlation, norm_sum = lax.psum(
        (jnp.sum(vector_rows * sigma_rows), jnp.sum(vector_rows * vector_rows)), ("ops", "sector")
    )
    rayleigh = correlation / norm_sum
    leftover = sigma_rows - rayleigh * vector_rows
    spread = lax.psum(jnp.sum(leftover * leftover), ("ops", "sector"))
    return (rayleigh, spread)


def on_device(psi, left_ops, right_ops, basis, block_dims):
    block_size = psi.shape[2]
    live = live_mask(block_dims, block_size)
    half_env = jnp.einsum(
        "ckqab,cqbd->ckqad", left_ops, basis, preferred_element_type=jnp.float32
    ).astype(jnp.bfloat16)
    boundary_ops = jnp.einsum(
        "cqba,ckqbd->ckqad", basis, half_env, preferred_element_type=jnp.float32
    ).astype(jnp.bfloat16)
    shifted = from_behind(boundary_ops, "chain", 1)
    vector = jnp.where(live > 0, psi, jnp.zeros_like(psi))
    entry_count = float(SECTORS * block_size * block_size)
    share_rows = block_size // lax.axis_size("ops")
    row_start = lax.axis_index("ops") * share_rows
    live_rows = lax.dynamic_slice_in_dim(live, row_start, share_rows, 2)
    residual = jnp.zeros(live_rows.shape, jnp.float32)
    quotients = []
    for iteration in range(ITERS):
        products = jnp.einsum(
            "ckqab,cqbd->ckqad", shifted, vector, preferred_element_type=jnp.float32
        ).astype(jnp.bfloat16)
        partial_sigma = jnp.einsum(
            "ckqad,ckqed->cqae", products, right_ops, preferred_element_type=jnp.float32
        )
        sigma_full = lax.psum(partial_sigma, "ops") * live
        sigma_rows = lax.dynamic_slice_in_dim(sigma_full, row_start, share_rows, 2)
        vector_rows = lax.dynamic_slice_in_dim(vector, row_start, share_rows, 2).astype(jnp.float32)
        rayleigh, spread = quotient(vector_rows, sigma_rows)
        quotients.append(rayleigh)
        if iteration + 1 < ITERS:
            residue = sigma_full - rayleigh * vector.astype(jnp.float32)
            vector = (residue * lax.rsqrt(spread / entry_count + 1e-06)).astype(jnp.bfloat16)
        else:
            residual = sigma_rows - rayleigh * vector_rows
    thetas = jnp.stack(quotients).reshape(1, ITERS)
    return (residual, thetas)


def solution(mesh):
    in_specs = (
        P("chain", "sector", None, None),
        P("chain", "ops", "sector", None, None),
        P("chain", "ops", "sector", None, None),
        P("chain", "sector", None, None),
        P("chain", "sector"),
    )
    out_specs = (P("chain", "sector", "ops", None), P("chain", None))
    return jax.shard_map(
        on_device, mesh=mesh, in_specs=in_specs, out_specs=out_specs, check_vma=False
    )
```

profile of v0, /device:TPU:0, one launch (start us, length us, event | category | flops | bytes accessed | tf_op | source)
XLA Modules:
  0.0 908.4 jit_solution(11232983917351738065)
XLA Ops:
  7.2 0.0 copy-start
  7.2 0.0 copy-start.7
  7.2 0.0 copy-start.4
  7.2 0.0 all-reduce.7.cloned.1.call-start
  7.2 1.2 copy-done
  8.4 21.1 %convert_bitcast_fusion = bf16[1,12,4,384,384]{3,4,1,2,0:T(8,128)(2,1)} fusion(bf16[1,4,384,384]{3,2,1,0:T(8,128)(2,1)S(1)} %copy-done, bf16[1,12,4,384,384]{4,3,2,1,0:T(8,128)(2,1)} %param.6), kind=kOutput, calls=%fused_computation.19 | convolution fusion | flops 10885791744 | bytes 29491200 | tf_op jit(solution)/shard_map/cqba,ckqbd->ckqad/dot_general | solution.py:39
  29.5 2.9 collective-permute-start
  32.4 0.0 copy-done.7
  32.4 0.1 iota_compare_fusion
  32.5 0.0 copy-done.4
  32.5 0.5 fusion.43
  33.0 303.8 %collective-permute-done = bf16[1,12,4,384,384]{3,4,1,2,0:T(8,128)(2,1)} collective-permute-done((bf16[1,12,4,384,384]{3,4,1,2,0:T(8,128)(2,1)}, bf16[1,12,4,384,384]{3,4,1,2,0:T(8,128)(2,1)}, u32[]{:S(2)}, u32[]{:S(2)}) %collective-permute-start) | collective-permute-done | bytes 14155808 | tf_op jit(solution)/shard_map/ppermute | solution.py:13
  336.8 20.1 %fusion.44 = f32[1,4,384,384]{3,2,1,0:T(8,128)} fusion(bf16[1,12,4,384,384]{3,4,1,2,0:T(8,128)(2,1)} %collective-permute-done, bf16[1,4,384,384]{3,2,1,0:T(8,128)(2,1)S(1)} %fusion.43, bf16[1,12,4,384,384]{4,3,2,1,0:T(8,128)(2,1)} %param.7), kind=kOutput, calls=%fused_computation.30 | convolution fusion | flops 10878713856 | bytes 31850496 | tf_op jit(solution)/shard_map/ckqad,ckqed->cqae/dot_general | solution.py:54
  356.9 0.0 all-reduce.7.cloned.1.call-update
  357.0 0.0 all-reduce.9.cloned.1.call-start
  357.0 110.3 %all-reduce.7.cloned.1.call-done = f32[1,4,384,384]{3,2,1,0:T(8,128)} async-done(((f32[1,4,384,384]{3,2,1,0:T(8,128)}), f32[1,4,384,384]{3,2,1,0:T(8,128)}) %all-reduce.7.cloned.1.call-update) | async-done | bytes 2359312 | tf_op jit(solution)/shard_map/psum | solution.py:57
  467.4 0.0 copy-start.2
  467.4 2.1 and_select_fusion.1
  469.5 0.0 copy-start.5
  469.5 1.4 copy-done.5
  470.9 0.7 fusion.74
  471.6 32.1 %all-reduce.2 = (f32[]{:T(128)}, f32[]{:T(128)}) all-reduce(f32[]{:T(128)} %get-tuple-element.7, f32[]{:T(128)} %get-tuple-element.6), channel_id=1, replica_groups=mesh['chain'=2,'ops'=8,'sector'=2] {'ops','sector'}, use_global_device_ids=true, to_apply=%region_2.3 | all-reduce | flops 2 | bytes 16 | tf_op jit(solution)/shard_map/psum | solution.py:24
  505.0 1.7 fusion.77
  506.7 30.3 %psum.80 = f32[]{:T(128)} all-reduce(f32[]{:T(128)} %fusion.77), channel_id=1, replica_groups=mesh['chain'=2,'ops'=8,'sector'=2] {'ops','sector'}, use_global_device_ids=true, to_apply=%region_6.7 | all-reduce | flops 1 | bytes 8 | tf_op jit(solution)/shard_map/psum | solution.py:29
  537.6 0.0 copy-done.2
  537.7 2.1 multiply_convert_fusion.1
  539.7 20.1 %fusion.51 = f32[1,4,384,384]{3,2,1,0:T(8,128)} fusion(bf16[1,12,4,384,384]{3,4,1,2,0:T(8,128)(2,1)} %collective-permute-done, bf16[1,4,384,384]{3,2,1,0:T(8,128)(2,1)S(1)} %multiply_convert_fusion.1, bf16[1,12,4,384,384]{4,3,2,1,0:T(8,128)(2,1)} %param.7), kind=kOutput, calls=%fused_computation.31 | convolution fusion | flops 10878713856 | bytes 31850496 | tf_op jit(solution)/shard_map/ckqad,ckqed->cqae/dot_general | solution.py:54
  559.9 0.0 all-reduce.9.cloned.1.call-update
  559.9 0.0 all-reduce.11.cloned.1.call-start
  559.9 106.1 %all-reduce.9.cloned.1.call-done = f32[1,4,384,384]{3,2,1,0:T(8,128)} async-done(((f32[1,4,384,384]{3,2,1,0:T(8,128)}), f32[1,4,384,384]{3,2,1,0:T(8,128)}) %all-reduce.9.cloned.1.call-update) | async-done | bytes 2359312 | tf_op jit(solution)/shard_map/psum | solution.py:57
  666.0 0.0 copy-start.3
  666.0 2.1 and_select_fusion
  668.1 0.0 copy-start.6
  668.1 1.4 copy-done.6
  669.6 0.7 fusion.79
  670.3 32.1 %all-reduce.1 = (f32[]{:T(128)}, f32[]{:T(128)}) all-reduce(f32[]{:T(128)} %get-tuple-element.5, f32[]{:T(128)} %get-tuple-element.4), channel_id=1, replica_groups=mesh['chain'=2,'ops'=8,'sector'=2] {'ops','sector'}, use_global_device_ids=true, to_apply=%region_9.10 | all-reduce | flops 2 | bytes 16 | tf_op jit(solution)/shard_map/psum | solution.py:24
  703.7 1.7 fusion.82
  705.3 30.1 %psum.84 = f32[]{:T(128)} all-reduce(f32[]{:T(128)} %fusion.82), channel_id=1, replica_groups=mesh['chain'=2,'ops'=8,'sector'=2] {'ops','sector'}, use_global_device_ids=true, to_apply=%region_13.14 | all-reduce | flops 1 | bytes 8 | tf_op jit(solution)/shard_map/psum | solution.py:29
  736.1 0.0 copy-done.3
  736.1 1.7 multiply_convert_fusion
  737.8 0.0 copy-start.1
  737.8 20.3 %fusion.58 = f32[1,4,384,384]{3,2,1,0:T(8,128)} fusion(bf16[1,12,4,384,384]{3,4,1,2,0:T(8,128)(2,1)} %collective-permute-done, bf16[1,4,384,384]{3,2,1,0:T(8,128)(2,1)} %multiply_convert_fusion, bf16[1,12,4,384,384]{4,3,2,1,0:T(8,128)(2,1)} %param.7), kind=kOutput, calls=%fused_computation.32 | convolution fusion | flops 10878713856 | bytes 31850496 | tf_op jit(solution)/shard_map/ckqad,ckqed->cqae/dot_general | solution.py:54
  758.1 0.0 all-reduce.11.cloned.1.call-update
  758.1 0.3 broadcast_and_fusion
  758.5 105.7 %all-reduce.11.cloned.1.call-done = f32[1,4,384,384]{3,2,1,0:T(8,128)} async-done(((f32[1,4,384,384]{3,2,1,0:T(8,128)}), f32[1,4,384,384]{3,2,1,0:T(8,128)}) %all-reduce.11.cloned.1.call-update) | async-done | bytes 2359312 | tf_op jit(solution)/shard_map/psum | solution.py:57
  864.2 1.8 fusion.84
  866.0 32.2 %all-reduce = (f32[]{:T(128)}, f32[]{:T(128)}) all-reduce(f32[]{:T(128)} %get-tuple-element.3, f32[]{:T(128)} %get-tuple-element.2), channel_id=1, replica_groups=mesh['chain'=2,'ops'=8,'sector'=2] {'ops','sector'}, use_global_device_ids=true, to_apply=%region_16.17 | all-reduce | flops 2 | bytes 16 | tf_op jit(solution)/shard_map/psum | solution.py:24
  899.5 0.6 maximum_bitcast_fusion
  900.1 1.8 fusion.85
  901.9 0.0 copy-done.1
Async XLA Ops:
  7.2 1.3 copy-start
  7.2 25.3 %copy-start.7 = (s32[1,4]{1,0:T(1,128)S(1)}, s32[1,4]{1,0:T(1,128)}, u32[]{:S(2)}) copy-start(s32[1,4]{1,0:T(1,128)} %param.9) | copy-start | bytes 52
  7.2 25.3 %copy-start.4 = (bf16[1,4,384,384]{3,2,1,0:T(8,128)(2,1)S(1)}, bf16[1,4,384,384]{3,2,1,0:T(8,128)(2,1)}, u32[]{:S(2)}) copy-start(bf16[1,4,384,384]{3,2,1,0:T(8,128)(2,1)} %param.5) | copy-start | bytes 3538948
  7.2 460.2 %all-reduce.7.cloned.1.call-start = ((), (), s32[]{:S(2)}) async-start(), calls=%async_computation | async-start | bytes 4718592 | tf_op jit(solution)/shard_map/psum | solution.py:57
  29.5 307.3 %collective-permute-start = (bf16[1,12,4,384,384]{3,4,1,2,0:T(8,128)(2,1)}, bf16[1,12,4,384,384]{3,4,1,2,0:T(8,128)(2,1)}, u32[]{:S(2)}, u32[]{:S(2)}) collective-permute-start(bf16[1,12,4,384,384]{3,4,1,2,0:T(8,128)(2,1)} %convert_bitcast_fusion), channel_id=1, source_target_pairs={{16,0},{0,16},{17,1},{1,17},{18,2},{2,18},{19,3},{3,19},{20,4},{4,... | collective-permute-start | bytes 42467336 | tf_op jit(solution)/shard_map/ppermute | solution.py:13
  357.0 309.0 %all-reduce.9.cloned.1.call-start = ((), (), s32[]{:S(2)}) async-start(), calls=%async_computation.1 | async-start | bytes 4718592 | tf_op jit(solution)/shard_map/psum | solution.py:57
  467.4 70.3 %copy-start.2 = (f32[1,4,384,384]{3,2,1,0:T(8,128)S(1)}, f32[1,4,384,384]{3,2,1,0:T(8,128)}, u32[]{:S(2)}) copy-start(f32[1,4,384,384]{3,2,1,0:T(8,128)} %all-reduce.7.cloned.1.call-done) | copy-start | bytes 7077892
  469.5 1.4 copy-start.5
  559.9 304.3 %all-reduce.11.cloned.1.call-start = ((), (), s32[]{:S(2)}) async-start(), calls=%async_computation.2 | async-start | bytes 4718592 | tf_op jit(solution)/shard_map/psum | solution.py:57
  666.0 70.1 %copy-start.3 = (f32[1,4,384,384]{3,2,1,0:T(8,128)S(1)}, f32[1,4,384,384]{3,2,1,0:T(8,128)}, u32[]{:S(2)}) copy-start(f32[1,4,384,384]{3,2,1,0:T(8,128)} %all-reduce.9.cloned.1.call-done) | copy-start | bytes 7077892
  668.1 1.4 copy-start.6
  737.8 164.1 %copy-start.1 = (bf16[1,4,384,384]{3,2,1,0:T(8,128)(2,1)S(1)}, bf16[1,4,384,384]{3,2,1,0:T(8,128)(2,1)}, u32[]{:S(2)}) copy-start(bf16[1,4,384,384]{3,2,1,0:T(8,128)(2,1)} %param.8) | copy-start | bytes 3538948
Sparse Core Ops, SparseCore 0:
  357.1 110.2 all-reduce.6
  560.0 105.9 all-reduce.8
  758.3 105.8 all-reduce.10
where the time goes:
time: 909 us; the launch traced here: 908 us
  waiting for transfers between devices  626 us (69%)
  blocking collectives  157 us (17%)
  matrix products  81.7 us (9%)
  between operations  19.3 us (2%)
  other arithmetic  17.8 us (2%)
    psum x3, waiting for transfers between devices, on_device(): sigma_full = lax.psum(partial_sigma, 'ops') * live  322 us
    ppermute x1, waiting for transfers between devices, from_behind(): return lax.ppermute(block, axis, route)  304 us
    psum x3, blocking collectives, quotient(): lax.psum((jnp.sum(vector_rows * sigma_rows), jnp.sum(vector_rows * vector...  96.3 us
    dot_general x3, matrix products, on_device(): jnp.einsum('ckqad,ckqed->cqae', products, right_ops, preferred_element_ty...  60.6 us
    psum x2, blocking collectives, quotient(): spread = lax.psum(jnp.sum(leftover * leftover), ('ops', 'sector'))  60.4 us
    dot_general x1, matrix products, on_device(): jnp.einsum('cqba,ckqbd->ckqad', basis, half_env, preferred_element_type=j...  21.1 us
  transfers between devices with their start and end apart: 4, of which 4 were waited for; matrix products, arithmetic and copies ran while one was open for 0% of the time, Pallas kernels for 0%

commit v1 on v0

--- a/solution.py
+++ b/solution.py
@@ -22,7 +22,8 @@
 
 def quotient(vector_rows, sigma_rows):
     correlation, norm_sum = lax.psum(
-        (jnp.sum(vector_rows * sigma_rows), jnp.sum(vector_rows * vector_rows)), ("ops", "sector")
+        lax.psum((jnp.sum(vector_rows * sigma_rows), jnp.sum(vector_rows * vector_rows)), "sector"),
+        "ops",
     )
     rayleigh = correlation / norm_sum
     leftover = sigma_rows - rayleigh * vector_rows

time: 909 us -> 882 us (0.970)
  blocking collectives: 157 us -> 130 us
    psum x3, blocking collectives: 96.3 us -> 9.34 us  [quotient(): lax.psum((jnp.sum(vector_rows * sigma_rows), jnp.sum(vector_rows * vector...]
    psum x0 -> x3, blocking collectives: none -> 60.4 us  [quotient(): lax.psum(lax.psum((jnp.sum(vector_rows * sigma_rows), jnp.sum(vector_rows...]
where the time goes in v1:
time: 882 us
  waiting for transfers between devices  626 us (71%)
  blocking collectives  130 us (15%)
  matrix products  81.7 us (9%)
  between operations  19.3 us (2%)
  other arithmetic  17.8 us (2%)
    psum x3, waiting for transfers between devices, on_device(): sigma_full = lax.psum(partial_sigma, 'ops') * live  322 us
    ppermute x1, waiting for transfers between devices, from_behind(): return lax.ppermute(block, axis, route)  304 us
    dot_general x3, matrix products, on_device(): jnp.einsum('ckqad,ckqed->cqae', products, right_ops, preferred_element_ty...  60.6 us
    psum x3, blocking collectives, quotient(): lax.psum(lax.psum((jnp.sum(vector_rows * sigma_rows), jnp.sum(vector_rows...  60.4 us
    psum x2, blocking collectives, quotient(): spread = lax.psum(jnp.sum(leftover * leftover), ('ops', 'sector'))  60.4 us
    dot_general x1, matrix products, on_device(): jnp.einsum('cqba,ckqbd->ckqad', basis, half_env, preferred_element_type=j...  21.1 us
  transfers between devices with their start and end apart: 4, of which 4 were waited for; matrix products, arithmetic and copies ran while one was open for 0% of the time, Pallas kernels for 0%

profile of v1, /device:TPU:0, one launch (start us, length us, event | category | flops | bytes accessed | tf_op | source)
XLA Modules:
  0.0 881.8 jit_solution(12792004924860882568)
XLA Ops:
  7.2 0.0 copy-start
  7.2 0.0 copy-start.7
  7.2 0.0 copy-start.4
  7.2 0.0 all-reduce.10.cloned.1.call-start
  7.2 1.2 copy-done
  8.4 21.1 %convert_bitcast_fusion = bf16[1,12,4,384,384]{3,4,1,2,0:T(8,128)(2,1)} fusion(bf16[1,4,384,384]{3,2,1,0:T(8,128)(2,1)S(1)} %copy-done, bf16[1,12,4,384,384]{4,3,2,1,0:T(8,128)(2,1)} %param.6), kind=kOutput, calls=%fused_computation.19 | convolution fusion | flops 10885791744 | bytes 29491200 | tf_op jit(solution)/shard_map/cqba,ckqbd->ckqad/dot_general | solution.py:40
  29.5 2.9 collective-permute-start
  32.4 0.0 copy-done.7
  32.4 0.1 iota_compare_fusion
  32.5 0.0 copy-done.4
  32.5 0.5 fusion.43
  33.0 303.8 %collective-permute-done = bf16[1,12,4,384,384]{3,4,1,2,0:T(8,128)(2,1)} collective-permute-done((bf16[1,12,4,384,384]{3,4,1,2,0:T(8,128)(2,1)}, bf16[1,12,4,384,384]{3,4,1,2,0:T(8,128)(2,1)}, u32[]{:S(2)}, u32[]{:S(2)}) %collective-permute-start) | collective-permute-done | bytes 14155808 | tf_op jit(solution)/shard_map/ppermute | solution.py:13
  336.8 20.1 %fusion.44 = f32[1,4,384,384]{3,2,1,0:T(8,128)} fusion(bf16[1,12,4,384,384]{3,4,1,2,0:T(8,128)(2,1)} %collective-permute-done, bf16[1,4,384,384]{3,2,1,0:T(8,128)(2,1)S(1)} %fusion.43, bf16[1,12,4,384,384]{4,3,2,1,0:T(8,128)(2,1)} %param.7), kind=kOutput, calls=%fused_computation.30 | convolution fusion | flops 10878713856 | bytes 31850496 | tf_op jit(solution)/shard_map/ckqad,ckqed->cqae/dot_general | solution.py:55
  356.9 0.0 all-reduce.10.cloned.1.call-update
  357.0 0.0 all-reduce.12.cloned.1.call-start
  357.0 110.3 %all-reduce.10.cloned.1.call-done = f32[1,4,384,384]{3,2,1,0:T(8,128)} async-done(((f32[1,4,384,384]{3,2,1,0:T(8,128)}), f32[1,4,384,384]{3,2,1,0:T(8,128)}) %all-reduce.10.cloned.1.call-update) | async-done | bytes 2359312 | tf_op jit(solution)/shard_map/psum | solution.py:58
  467.4 0.0 copy-start.2
  467.4 2.1 and_select_fusion.1
  469.5 0.0 copy-start.5
  469.5 1.4 copy-done.5
  470.9 0.7 fusion.74
  471.6 3.1 all-reduce.5
  474.7 20.1 %all-reduce.2 = (f32[]{:T(128)}, f32[]{:T(128)}) all-reduce(f32[]{:T(128)} %get-tuple-element.18, f32[]{:T(128)} %get-tuple-element.19), channel_id=1, replica_groups=mesh['chain'=2,'ops'=8,'sector'=2] {'ops'}, use_global_device_ids=true, to_apply=%region_3.4 | all-reduce | flops 2 | bytes 16 | tf_op jit(solution)/shard_map/psum | solution.py:24
  496.1 1.7 fusion.77
  497.8 30.3 %psum.124 = f32[]{:T(128)} all-reduce(f32[]{:T(128)} %fusion.77), channel_id=1, replica_groups=mesh['chain'=2,'ops'=8,'sector'=2] {'ops','sector'}, use_global_device_ids=true, to_apply=%region_8.9 | all-reduce | flops 1 | bytes 8 | tf_op jit(solution)/shard_map/psum | solution.py:30
  528.8 0.0 copy-done.2
  528.8 2.1 multiply_convert_fusion.1
  530.8 20.1 %fusion.51 = f32[1,4,384,384]{3,2,1,0:T(8,128)} fusion(bf16[1,12,4,384,384]{3,4,1,2,0:T(8,128)(2,1)} %collective-permute-done, bf16[1,4,384,384]{3,2,1,0:T(8,128)(2,1)S(1)} %multiply_convert_fusion.1, bf16[1,12,4,384,384]{4,3,2,1,0:T(8,128)(2,1)} %param.7), kind=kOutput, calls=%fused_computation.31 | convolution fusion | flops 10878713856 | bytes 31850496 | tf_op jit(solution)/shard_map/ckqad,ckqed->cqae/dot_general | solution.py:55
  551.0 0.0 all-reduce.12.cloned.1.call-update
  551.0 0.0 all-reduce.14.cloned.1.call-start
  551.1 106.0 %all-reduce.12.cloned.1.call-done = f32[1,4,384,384]{3,2,1,0:T(8,128)} async-done(((f32[1,4,384,384]{3,2,1,0:T(8,128)}), f32[1,4,384,384]{3,2,1,0:T(8,128)}) %all-reduce.12.cloned.1.call-update) | async-done | bytes 2359312 | tf_op jit(solution)/shard_map/psum | solution.py:58
  657.1 0.0 copy-start.3
  657.1 2.1 and_select_fusion
  659.2 0.0 copy-start.6
  659.2 1.4 copy-done.6
  660.6 0.7 fusion.79
  661.3 3.1 all-reduce.4
  664.5 20.1 %all-reduce.1 = (f32[]{:T(128)}, f32[]{:T(128)}) all-reduce(f32[]{:T(128)} %get-tuple-element.16, f32[]{:T(128)} %get-tuple-element.17), channel_id=1, replica_groups=mesh['chain'=2,'ops'=8,'sector'=2] {'ops'}, use_global_device_ids=true, to_apply=%region_12.13 | all-reduce | flops 2 | bytes 16 | tf_op jit(solution)/shard_map/psum | solution.py:24
  685.9 1.7 fusion.82
  687.5 30.1 %psum.130 = f32[]{:T(128)} all-reduce(f32[]{:T(128)} %fusion.82), channel_id=1, replica_groups=mesh['chain'=2,'ops'=8,'sector'=2] {'ops','sector'}, use_global_device_ids=true, to_apply=%region_17.18 | all-reduce | flops 1 | bytes 8 | tf_op jit(solution)/shard_map/psum | solution.py:30
  718.3 0.0 copy-done.3
  718.3 1.7 multiply_convert_fusion
  720.0 0.0 copy-start.1
  720.0 20.3 %fusion.58 = f32[1,4,384,384]{3,2,1,0:T(8,128)} fusion(bf16[1,12,4,384,384]{3,4,1,2,0:T(8,128)(2,1)} %collective-permute-done, bf16[1,4,384,384]{3,2,1,0:T(8,128)(2,1)} %multiply_convert_fusion, bf16[1,12,4,384,384]{4,3,2,1,0:T(8,128)(2,1)} %param.7), kind=kOutput, calls=%fused_computation.32 | convolution fusion | flops 10878713856 | bytes 31850496 | tf_op jit(solution)/shard_map/ckqad,ckqed->cqae/dot_general | solution.py:55
  740.3 0.0 all-reduce.14.cloned.1.call-update
  740.3 0.3 broadcast_and_fusion
  740.7 105.7 %all-reduce.14.cloned.1.call-done = f32[1,4,384,384]{3,2,1,0:T(8,128)} async-done(((f32[1,4,384,384]{3,2,1,0:T(8,128)}), f32[1,4,384,384]{3,2,1,0:T(8,128)}) %all-reduce.14.cloned.1.call-update) | async-done | bytes 2359312 | tf_op jit(solution)/shard_map/psum | solution.py:58
  846.4 1.8 fusion.84
  848.2 3.1 all-reduce.3
  851.4 20.2 %all-reduce = (f32[]{:T(128)}, f32[]{:T(128)}) all-reduce(f32[]{:T(128)} %get-tuple-element.14, f32[]{:T(128)} %get-tuple-element.15), channel_id=1, replica_groups=mesh['chain'=2,'ops'=8,'sector'=2] {'ops'}, use_global_device_ids=true, to_apply=%region_21.22 | all-reduce | flops 2 | bytes 16 | tf_op jit(solution)/shard_map/psum | solution.py:24
  872.9 0.6 maximum_bitcast_fusion
  873.5 1.8 fusion.85
  875.3 0.0 copy-done.1
Async XLA Ops:
  7.2 1.3 copy-start
  7.2 25.3 %copy-start.7 = (s32[1,4]{1,0:T(1,128)S(1)}, s32[1,4]{1,0:T(1,128)}, u32[]{:S(2)}) copy-start(s32[1,4]{1,0:T(1,128)} %param.9) | copy-start | bytes 52
  7.2 25.3 %copy-start.4 = (bf16[1,4,384,384]{3,2,1,0:T(8,128)(2,1)S(1)}, bf16[1,4,384,384]{3,2,1,0:T(8,128)(2,1)}, u32[]{:S(2)}) copy-start(bf16[1,4,384,384]{3,2,1,0:T(8,128)(2,1)} %param.5) | copy-start | bytes 3538948
  7.2 460.2 %all-reduce.10.cloned.1.call-start = ((), (), s32[]{:S(2)}) async-start(), calls=%async_computation | async-start | bytes 4718592 | tf_op jit(solution)/shard_map/psum | solution.py:58
  29.5 307.3 %collective-permute-start = (bf16[1,12,4,384,384]{3,4,1,2,0:T(8,128)(2,1)}, bf16[1,12,4,384,384]{3,4,1,2,0:T(8,128)(2,1)}, u32[]{:S(2)}, u32[]{:S(2)}) collective-permute-start(bf16[1,12,4,384,384]{3,4,1,2,0:T(8,128)(2,1)} %convert_bitcast_fusion), channel_id=1, source_target_pairs={{16,0},{0,16},{17,1},{1,17},{18,2},{2,18},{19,3},{3,19},{20,4},{4,... | collective-permute-start | bytes 42467336 | tf_op jit(solution)/shard_map/ppermute | solution.py:13
  357.0 300.1 %all-reduce.12.cloned.1.call-start = ((), (), s32[]{:S(2)}) async-start(), calls=%async_computation.1 | async-start | bytes 4718592 | tf_op jit(solution)/shard_map/psum | solution.py:58
  467.4 61.4 %copy-start.2 = (f32[1,4,384,384]{3,2,1,0:T(8,128)S(1)}, f32[1,4,384,384]{3,2,1,0:T(8,128)}, u32[]{:S(2)}) copy-start(f32[1,4,384,384]{3,2,1,0:T(8,128)} %all-reduce.10.cloned.1.call-done) | copy-start | bytes 7077892
  469.5 1.4 copy-start.5
  551.0 295.4 %all-reduce.14.cloned.1.call-start = ((), (), s32[]{:S(2)}) async-start(), calls=%async_computation.2 | async-start | bytes 4718592 | tf_op jit(solution)/shard_map/psum | solution.py:58
  657.1 61.2 %copy-start.3 = (f32[1,4,384,384]{3,2,1,0:T(8,128)S(1)}, f32[1,4,384,384]{3,2,1,0:T(8,128)}, u32[]{:S(2)}) copy-start(f32[1,4,384,384]{3,2,1,0:T(8,128)} %all-reduce.12.cloned.1.call-done) | copy-start | bytes 7077892
  659.2 1.4 copy-start.6
  720.0 155.3 %copy-start.1 = (bf16[1,4,384,384]{3,2,1,0:T(8,128)(2,1)S(1)}, bf16[1,4,384,384]{3,2,1,0:T(8,128)(2,1)}, u32[]{:S(2)}) copy-start(bf16[1,4,384,384]{3,2,1,0:T(8,128)(2,1)} %param.8) | copy-start | bytes 3538948
Sparse Core Ops, SparseCore 0:
  357.1 110.2 all-reduce.9
  551.1 105.9 all-reduce.11
  740.5 105.9 all-reduce.13
